TPU v7x, 512 devices: a whole 4x4x16 slice. The times are simulated.
512 devices in a mesh: ctx: 64 (over x, z_lo, core), head: 8 (over y, z_hi).
Axes of the slice: x: 4, y: 4, z: 16 (z_hi: 2, z_lo: 8; z = z_hi * 8 + z_lo), core: 2. Of those that a mesh axis runs over, the one named last changes fastest.
Arguments:
- queries: bfloat16 [16384, 2048], P('ctx', 'head'), may hold values from -40 to 40
- keys: bfloat16 [16384, 2048], P('ctx', 'head'), may hold values from -4 to 4
- values: bfloat16 [16384, 2048], P('ctx', 'head'), may hold values from -5 to 5
- selected: int32 [16, 512, 3], P('head', 'ctx'), may hold values from 0 to 63, as said below
- out_weight: bfloat16 [2048, 2048], P(None, 'head'), may hold values from -0.125 to 0.125
Outputs:
- projected: bfloat16 [16384, 2048], P('ctx', 'head')
Inputs may be any that keep to these rules, and one draw needn't show every extreme that they name: `selected`: entry 0 of a tile's selection is its own block; entries 1 and 2 are two different earlier blocks, or both the own block where no earlier block is chosen for the tile (one earlier block and the own block in the second key block). For each head, the tiles of one key block name any one other block at most 2 times, and exactly 2 times for every block they name, from the third key block on.
All inputs are finite; a program needn't handle non-finite values.
Results may differ from a plain program's by a relative error of at most 0.0054.
Values may be sent and summed in bfloat16 or wider, within the bound.
No kernel may reach another device: no remote copies, remote signals or barrier semaphores. Data moves between devices by JAX's collectives and lax.ppermute only.
A program may use at most 64 MiB of HBM per device.

v0:
```python
import math
import jax
import jax.numpy as jnp
from jax import lax
from jax.sharding import PartitionSpec as P

CAP = 2


def owner_block(group, keys_three, vals_three, scale):
    scores = (
        jnp.einsum("gchtd,khd->gchtk", group, keys_three, preferred_element_type=jnp.float32)
        * scale
    )
    top = jnp.max(scores, axis=-1)
    prob = jnp.exp(scores - top[..., None])
    total = jnp.sum(prob, axis=-1)
    part = jnp.einsum(
        "gchtk,khd->gchtd",
        prob.astype(jnp.bfloat16),
        vals_three,
        preferred_element_type=jnp.float32,
    )
    return (part / total[..., None], top + jnp.log(total))


def partials_back(outputs, sums):
    return (
        lax.all_to_all(outputs, "ctx", split_axis=0, concat_axis=0, tiled=True),
        lax.all_to_all(sums, "ctx", split_axis=0, concat_axis=0, tiled=True),
    )


def group_size(sources, rows_each):
    size = max(1, 512 // rows_each)
    size = min(size, sources)
    while sources % size != 0:
        size = size - 1
    return size


def local(queries, keys, values, selected, out_weight):
    heads_loc = selected.shape[0]
    tiles = selected.shape[1]
    tokens_here = queries.shape[0]
    width = queries.shape[1] // heads_loc
    tile_rows = tokens_here // tiles
    sources = lax.axis_size("ctx")
    mine = lax.axis_index("ctx")
    scale = width ** (-0.5)
    quer_three = queries.reshape(tokens_here, heads_loc, width)
    keys_three = keys.reshape(tokens_here, heads_loc, width)
    vals_three = values.reshape(tokens_here, heads_loc, width)
    rows_blk = math.gcd(tokens_here, 512)
    row_groups = tokens_here // rows_blk
    key_pos = jnp.arange(tokens_here, dtype=jnp.int32)

    def own_rows(args):
        query_rows, start = args
        scores = (
            jnp.einsum("rhd,khd->hrk", query_rows, keys_three, preferred_element_type=jnp.float32)
            * scale
        )
        allowed = (start + jnp.arange(rows_blk, dtype=jnp.int32))[:, None] >= key_pos[None, :]
        scores = jnp.where(allowed[None], scores, jnp.float32(-1e30))
        top = jnp.max(scores, axis=-1)
        prob = jnp.exp(scores - top[..., None])
        total = jnp.sum(prob, axis=-1)
        part = jnp.einsum(
            "hrk,khd->hrd",
            prob.astype(jnp.bfloat16),
            vals_three,
            preferred_element_type=jnp.float32,
        )
        return (part / total[..., None], top + jnp.log(total))

    own_out, own_lse = lax.map(
        own_rows,
        (
            quer_three.reshape(row_groups, rows_blk, heads_loc, width),
            jnp.arange(row_groups, dtype=jnp.int32) * rows_blk,
        ),
    )
    own_out = jnp.transpose(own_out, (1, 0, 2, 3)).reshape(heads_loc, tiles, tile_rows, width)
    own_lse = jnp.transpose(own_lse, (1, 0, 2)).reshape(heads_loc, tiles, tile_rows)
    picks = selected[:, :, 1:]
    valid = picks != mine
    target = jnp.where(valid, picks, sources)
    onehot = (target[..., None] == jnp.arange(sources, dtype=jnp.int32)).astype(jnp.int32)
    flat_hot = onehot.reshape(heads_loc, tiles * 2, sources)
    before = jnp.cumsum(flat_hot, axis=1) - flat_hot
    slot = jnp.sum(before * flat_hot, axis=-1).reshape(heads_loc, tiles, 2)
    head_idx = jnp.broadcast_to(
        jnp.arange(heads_loc, dtype=jnp.int32)[:, None, None], (heads_loc, tiles, 2)
    )
    query_src = jnp.transpose(quer_three.reshape(tiles, tile_rows, heads_loc, width), (2, 0, 1, 3))
    query_pairs = jnp.broadcast_to(query_src[:, :, None], (heads_loc, tiles, 2, tile_rows, width))
    send_q = jnp.zeros((sources, CAP, heads_loc, tile_rows, width), jnp.bfloat16)
    send_q = send_q.at[target, slot, head_idx].set(query_pairs, mode="drop")
    got_rows = lax.all_to_all(send_q, "ctx", split_axis=0, concat_axis=0, tiled=True)
    count = got_rows.shape[1]
    group_count = group_size(sources, count * heads_loc * tile_rows)
    query_groups = got_rows.reshape(
        sources // group_count, group_count, count, heads_loc, tile_rows, width
    )

    def one_group(group):
        return owner_block(group, keys_three, vals_three, scale)

    outputs, sums = lax.map(one_group, query_groups)
    got_out, got_lse = partials_back(
        outputs.reshape(sources, count, heads_loc, tile_rows, width),
        sums.reshape(sources, count, heads_loc, tile_rows),
    )
    clipped = jnp.clip(target, 0, sources - 1)
    pick_out = got_out[clipped, slot, head_idx]
    pick_lse = got_lse[clipped, slot, head_idx]
    keep = valid[..., None]
    top = jnp.maximum(own_lse, jnp.max(jnp.where(keep, pick_lse, own_lse[:, :, None]), axis=2))
    own_w = jnp.exp(own_lse - top)
    pick_w = jnp.exp(jnp.where(keep, pick_lse - top[:, :, None], jnp.float32(-1e30)))
    numer = own_w[..., None] * own_out + jnp.sum(pick_w[..., None] * pick_out, axis=2)
    denom = own_w + jnp.sum(pick_w, axis=2)
    attention = jnp.transpose(numer / denom[..., None], (1, 2, 0, 3)).reshape(
        tokens_here, heads_loc * width
    )
    attention = attention.astype(jnp.bfloat16)
    projected = jnp.dot(
        lax.all_gather(attention, "head", axis=1, tiled=True),
        out_weight,
        preferred_element_type=jnp.float32,
    )
    return projected.astype(jnp.bfloat16)


def solution(mesh):
    return jax.shard_map(
        local,
        mesh=mesh,
        in_specs=(
            P("ctx", "head"),
            P("ctx", "head"),
            P("ctx", "head"),
            P("head", "ctx", None),
            P(None, "head"),
        ),
        out_specs=P("ctx", "head"),
        check_vma=False,
    )
```

profile of v0, /device:TPU:2, one launch (start us, length us, event | category | flops | bytes accessed | tf_op | source)
XLA Modules:
  0.0 489.7 jit_solution(11999929789895695316)
XLA Ops:
  6.5 0.8 fusion.23
  8.2 0.9 reshape_reshape.4
  9.2 1.9 broadcast_in_dim.120
  11.1 4.2 scatter_fusion
  15.2 16.1 %all-to-all-start = ((bf16[64,2,2,32,128]{4,3,2,1,0:T(8,128)(2,1)}), bf16[64,2,2,32,128]{4,3,2,1,0:T(8,128)(2,1)S(1)}, u32[]{:S(2)}, u32[]{:S(2)}) async-start(bf16[64,2,2,32,128]{4,3,2,1,0:T(8,128)(2,1)} %scatter_fusion), calls=%async_computation | async-start | bytes 4194304 | tf_op jit(solution)/shard_map/all_to_all | solution.py:100
  31.6 1.0 copy.55
  32.6 0.7 copy.58
  33.3 92.5 %all-to-all-done = bf16[64,2,2,32,128]{4,3,2,1,0:T(8,128)(2,1)S(1)} async-done(((bf16[64,2,2,32,128]{4,3,2,1,0:T(8,128)(2,1)}), bf16[64,2,2,32,128]{4,3,2,1,0:T(8,128)(2,1)S(1)}, u32[]{:S(2)}, u32[]{:S(2)}) %all-to-all-start) | async-done | bytes 2097184 | tf_op jit(solution)/shard_map/all_to_all | solution.py:100
  125.9 50.5 %while.2 = (s32[]{:T(128)}, f32[16,4,2,2,32,128]{5,4,3,2,1,0:T(8,128)}, f32[16,4,2,2,32]{4,3,2,1,0:T(2,128)}, bf16[16,4,2,2,32,128]{5,4,3,2,1,0:T(8,128)(2,1)S(1...) while((s32[]{:T(128)}, f32[16,4,2,2,32,128]{5,4,3,2,1,0:T(8,128)}, ...), condition=%wide.region_8.9_spmd, body=%wide.region_5.8_spmd.sunk | while | flops 67960320 | bytes 2779233 | solution.py:110
  126.5 1.2 fusion.42
  129.6 1.2 fusion.42
  132.8 1.2 fusion.42
  135.9 1.2 fusion.42
  139.1 1.2 fusion.42
  142.2 1.2 fusion.42
  145.4 1.2 fusion.42
  148.6 1.2 fusion.42
  151.7 1.2 fusion.42
  154.9 1.2 fusion.42
  158.0 1.2 fusion.42
  161.2 1.2 fusion.42
  164.4 1.2 fusion.42
  167.5 1.2 fusion.42
  170.7 1.2 fusion.42
  173.8 1.2 fusion.42
  176.4 1.1 reshape.180
  177.5 21.2 %all_to_all.15 = f32[64,1,128]{2,1,0:T(1,128)S(1)} all-to-all(f32[64,1,128]{2,1,0:T(1,128)S(1)} %reshape.180), channel_id=1, replica_groups=mesh['ctx'=64,'head'=8] {'ctx'}, dimensions={0} | all-to-all | bytes 65536 | tf_op jit(solution)/shard_map/all_to_all | solution.py:30
  198.6 6.6 %all-to-all-start.2 = ((f32[64,2,2,32,128]{4,3,2,1,0:T(8,128)}), f32[64,2,2,32,128]{4,3,2,1,0:T(8,128)}, u32[]{:S(2)}, u32[]{:S(2)}) async-start(f32[64,2,2,32,128]{4,3,2,1,0:T(8,128)} %bitcast.87), calls=%async_computation.2 | async-start | bytes 8388608 | tf_op jit(solution)/shard_map/all_to_all | solution.py:29
  208.8 178.8 %all-to-all-done.2 = f32[64,2,2,32,128]{4,3,2,1,0:T(8,128)} async-done(((f32[64,2,2,32,128]{4,3,2,1,0:T(8,128)}), f32[64,2,2,32,128]{4,3,2,1,0:T(8,128)}, u32[]{:S(2)}, u32[]{:S(2)}) %all-to-all-start.2) | async-done | bytes 4194336 | tf_op jit(solution)/shard_map/all_to_all | solution.py:29
  387.6 2.8 gather_fusion.1
  391.7 88.8 %all-gather.2.cloned.1.call-done = bf16[256,2048]{1,0:T(8,128)(2,1)} async-done(((bf16[256,256]{1,0:T(8,128)(2,1)}), bf16[256,2048]{1,0:T(8,128)(2,1)}) %all-gather.2.cloned.1.call-update) | async-done | bytes 1048592 | tf_op jit(solution)/shard_map/all_gather | solution.py:129
  480.5 2.3 convolution_convert_fusion
  (126 shorter events, 36.9 us)
Async XLA Ops:
  6.5 474.0 %copy-start = (bf16[2048,256]{1,0:T(8,128)(2,1)S(1)}, bf16[2048,256]{1,0:T(8,128)(2,1)}, u32[]{:S(2)}) copy-start(bf16[2048,256]{1,0:T(8,128)(2,1)} %param.11) | copy-start | bytes 3145732
  6.5 24.8 %copy-start.2 = (bf16[256,256]{1,0:T(8,128)(2,1)S(1)}, bf16[256,256]{1,0:T(8,128)(2,1)}, u32[]{:S(2)}) copy-start(bf16[256,256]{1,0:T(8,128)(2,1)} %param.8) | copy-start | bytes 393220
  15.2 110.6 %all-to-all-start = ((bf16[64,2,2,32,128]{4,3,2,1,0:T(8,128)(2,1)}), bf16[64,2,2,32,128]{4,3,2,1,0:T(8,128)(2,1)S(1)}, u32[]{:S(2)}, u32[]{:S(2)}) async-start(bf16[64,2,2,32,128]{4,3,2,1,0:T(8,128)(2,1)} %scatter_fusion), calls=%async_computation | async-start | bytes 4194304 | tf_op jit(solution)/shard_map/all_to_all | solution.py:100
  198.6 7.0 %copy-start.1 = (bf16[256,256]{1,0:T(8,128)(2,1)S(1)}, bf16[256,256]{1,0:T(8,128)(2,1)}, u32[]{:S(2)}) copy-start(bf16[256,256]{1,0:T(8,128)(2,1)} %param.7) | copy-start | bytes 393220
  198.6 189.0 %all-to-all-start.2 = ((f32[64,2,2,32,128]{4,3,2,1,0:T(8,128)}), f32[64,2,2,32,128]{4,3,2,1,0:T(8,128)}, u32[]{:S(2)}, u32[]{:S(2)}) async-start(f32[64,2,2,32,128]{4,3,2,1,0:T(8,128)} %bitcast.87), calls=%async_computation.2 | async-start | bytes 8388608 | tf_op jit(solution)/shard_map/all_to_all | solution.py:29
  205.2 275.3 %all-gather.2.cloned.1.call-start = ((), (), s32[]{:S(2)}) async-start(), calls=%async_computation.3 | async-start | bytes 1179648 | tf_op jit(solution)/shard_map/all_gather | solution.py:129
Sparse Core Ops, SparseCore 0:
  391.8 88.6 all-gather.1
where the time goes:
time: 491 us; the launch traced here: 490 us
  waiting for transfers between devices  360 us (73%)
  local copies, waits for them, and re-layouts  37.3 us (8%)
  matrix products  26.9 us (5%)
  starting transfers between devices  22.7 us (5%)
  blocking collectives  21.2 us (4%)
  between operations  13.6 us (3%)
  other arithmetic  7.41 us (2%)
    all_to_all x1, waiting for transfers between devices, partials_back(): lax.all_to_all(outputs, 'ctx', split_axis=0, concat_axis=0, tiled=True)  179 us
    all_to_all x1, waiting for transfers between devices, local(): lax.all_to_all(send_q, 'ctx', split_axis=0, concat_axis=0, tiled=True)  92.5 us
    all_gather x1, waiting for transfers between devices, local(): lax.all_gather(attention, 'head', axis=1, tiled=True)  88.8 us
    dynamic_update_slice x32, local copies, waits for them, and re-layouts, local(): outputs, sums = lax.map(one_group, query_groups)  21.3 us
    all_to_all x1, blocking collectives, partials_back(): lax.all_to_all(sums, 'ctx', split_axis=0, concat_axis=0, tiled=True)  21.2 us
    dot_general x16, matrix products, owner_block(): jnp.einsum('gchtk,khd->gchtd', prob.astype(jnp.bfloat16), vals_three, pre...  19.1 us
    all_to_all x1, starting transfers between devices, local(): lax.all_to_all(send_q, 'ctx', split_axis=0, concat_axis=0, tiled=True)  16.1 us
  transfers between devices with their start and end apart: 3, of which 3 were waited for; matrix products, arithmetic and copies ran while one was open for 1% of the time, Pallas kernels for 0%

commit v1 on v0

--- a/solution.py
+++ b/solution.py
@@ -126,7 +126,12 @@
     )
     attention = attention.astype(jnp.bfloat16)
     projected = jnp.dot(
-        lax.all_gather(attention, "head", axis=1, tiled=True),
+        jnp.concatenate(
+            lax.all_to_all(
+                jnp.stack([attention for _ in range(lax.axis_size("head"))], 0), "head", 0, 0
+            ),
+            1,
+        ),
         out_weight,
         preferred_element_type=jnp.float32,
     )

time: 491 us -> 452 us (0.921)
  the two profiles are of different devices: /device:TPU:2 before, /device:TPU:7 now
where the time goes in v1:
time: 452 us
  waiting for transfers between devices  276 us (61%)
  blocking collectives  80.6 us (18%)
  local copies, waits for them, and re-layouts  36.8 us (8%)
  matrix products  25.8 us (6%)
  starting transfers between devices  24.4 us (5%)
  other arithmetic  7.41 us (2%)
    all_to_all x1, waiting for transfers between devices, partials_back(): lax.all_to_all(outputs, 'ctx', split_axis=0, concat_axis=0, tiled=True)  182 us
    all_to_all x1, waiting for transfers between devices, local(): lax.all_to_all(send_q, 'ctx', split_axis=0, concat_axis=0, tiled=True)  93.8 us
    all_to_all x1, blocking collectives, local(): lax.all_to_all(jnp.stack([attention for _ in range(lax.axis_size('head'))...  62 us
    dynamic_update_slice x32, local copies, waits for them, and re-layouts, local(): outputs, sums = lax.map(one_group, query_groups)  21.3 us
    dot_general x16, matrix products, owner_block(): jnp.einsum('gchtk,khd->gchtd', prob.astype(jnp.bfloat16), vals_three, pre...  19 us
    all_to_all x1, blocking collectives, partials_back(): lax.all_to_all(sums, 'ctx', split_axis=0, concat_axis=0, tiled=True)  18.6 us
    all_to_all x1, starting transfers between devices, local(): lax.all_to_all(send_q, 'ctx', split_axis=0, concat_axis=0, tiled=True)  16.5 us
  transfers between devices with their start and end apart: 2, of which 2 were waited for; matrix products, arithmetic and copies ran while one was open for 1% of the time, Pallas kernels for 0%

profile of v1, /device:TPU:7, one launch (start us, length us, event | category | flops | bytes accessed | tf_op | source)
XLA Modules:
  0.0 451.6 jit_solution(241048697076032231)
XLA Ops:
  0.0 0.8 fusion.23
  1.6 0.9 reshape_reshape.4
  2.7 1.9 broadcast_in_dim.120
  4.5 4.2 scatter_fusion
  8.7 16.5 %all-to-all-start = ((bf16[64,2,2,32,128]{4,3,2,1,0:T(8,128)(2,1)}), bf16[64,2,2,32,128]{4,3,2,1,0:T(8,128)(2,1)S(1)}, u32[]{:S(2)}, u32[]{:S(2)}) async-start(bf16[64,2,2,32,128]{4,3,2,1,0:T(8,128)(2,1)} %scatter_fusion), calls=%async_computation | async-start | bytes 4194304 | tf_op jit(solution)/shard_map/all_to_all | solution.py:100
  25.5 1.0 copy.56
  26.5 0.7 copy.59
  27.2 93.8 %all-to-all-done = bf16[64,2,2,32,128]{4,3,2,1,0:T(8,128)(2,1)S(1)} async-done(((bf16[64,2,2,32,128]{4,3,2,1,0:T(8,128)(2,1)}), bf16[64,2,2,32,128]{4,3,2,1,0:T(8,128)(2,1)S(1)}, u32[]{:S(2)}, u32[]{:S(2)}) %all-to-all-start) | async-done | bytes 2097184 | tf_op jit(solution)/shard_map/all_to_all | solution.py:100
  121.0 50.5 %while.2 = (s32[]{:T(128)}, f32[16,4,2,2,32,128]{5,4,3,2,1,0:T(8,128)}, f32[16,4,2,2,32]{4,3,2,1,0:T(2,128)}, bf16[16,4,2,2,32,128]{5,4,3,2,1,0:T(8,128)(2,1)S(1...) while((s32[]{:T(128)}, f32[16,4,2,2,32,128]{5,4,3,2,1,0:T(8,128)}, ...), condition=%wide.region_8.9_spmd, body=%wide.region_5.8_spmd.sunk | while | flops 67960320 | bytes 2779233 | solution.py:110
  121.6 1.2 fusion.42
  124.8 1.2 fusion.42
  127.9 1.2 fusion.42
  131.1 1.2 fusion.42
  134.2 1.2 fusion.42
  137.4 1.2 fusion.42
  140.6 1.2 fusion.42
  143.7 1.2 fusion.42
  146.9 1.2 fusion.42
  150.0 1.2 fusion.42
  153.2 1.2 fusion.42
  156.3 1.2 fusion.42
  159.5 1.2 fusion.42
  162.7 1.2 fusion.42
  165.8 1.2 fusion.42
  169.0 1.2 fusion.42
  171.5 1.1 reshape.191
  172.6 18.6 %all_to_all.20 = f32[64,1,128]{2,1,0:T(1,128)S(1)} all-to-all(f32[64,1,128]{2,1,0:T(1,128)S(1)} %reshape.191), channel_id=1, replica_groups=mesh['ctx'=64,'head'=8] {'ctx'}, dimensions={0} | all-to-all | bytes 65536 | tf_op jit(solution)/shard_map/all_to_all | solution.py:30
  191.2 7.9 %all-to-all-start.2 = ((f32[64,2,2,32,128]{4,3,2,1,0:T(8,128)}), f32[64,2,2,32,128]{4,3,2,1,0:T(8,128)}, u32[]{:S(2)}, u32[]{:S(2)}) async-start(f32[64,2,2,32,128]{4,3,2,1,0:T(8,128)} %bitcast.90), calls=%async_computation.2 | async-start | bytes 8388608 | tf_op jit(solution)/shard_map/all_to_all | solution.py:29
  202.6 182.2 %all-to-all-done.2 = f32[64,2,2,32,128]{4,3,2,1,0:T(8,128)} async-done(((f32[64,2,2,32,128]{4,3,2,1,0:T(8,128)}), f32[64,2,2,32,128]{4,3,2,1,0:T(8,128)}, u32[]{:S(2)}, u32[]{:S(2)}) %all-to-all-start.2) | async-done | bytes 4194336 | tf_op jit(solution)/shard_map/all_to_all | solution.py:29
  384.8 2.8 gather_fusion.1
  388.5 62.0 %all_to_all.21 = bf16[8,256,256]{1,2,0:T(8,128)(2,1)S(1)} all-to-all(bf16[8,256,256]{1,2,0:T(8,128)(2,1)S(1)} %stack.2), channel_id=1, replica_groups=mesh['ctx'=64,'head'=8] {'head'}, dimensions={0} | all-to-all | bytes 2097152 | tf_op jit(solution)/shard_map/all_to_all | solution.py:130
  450.4 1.1 convolution_convert_fusion
  (126 shorter events, 36.4 us)
Async XLA Ops:
  0.0 450.4 %copy-start = (bf16[2048,256]{1,0:T(8,128)(2,1)S(1)}, bf16[2048,256]{1,0:T(8,128)(2,1)}, u32[]{:S(2)}) copy-start(bf16[2048,256]{1,0:T(8,128)(2,1)} %param.11) | copy-start | bytes 3145732
  0.0 25.2 %copy-start.2 = (bf16[256,256]{1,0:T(8,128)(2,1)S(1)}, bf16[256,256]{1,0:T(8,128)(2,1)}, u32[]{:S(2)}) copy-start(bf16[256,256]{1,0:T(8,128)(2,1)} %param.8) | copy-start | bytes 393220
  8.7 112.3 %all-to-all-start = ((bf16[64,2,2,32,128]{4,3,2,1,0:T(8,128)(2,1)}), bf16[64,2,2,32,128]{4,3,2,1,0:T(8,128)(2,1)S(1)}, u32[]{:S(2)}, u32[]{:S(2)}) async-start(bf16[64,2,2,32,128]{4,3,2,1,0:T(8,128)(2,1)} %scatter_fusion), calls=%async_computation | async-start | bytes 4194304 | tf_op jit(solution)/shard_map/all_to_all | solution.py:100
  191.2 8.3 %copy-start.1 = (bf16[256,256]{1,0:T(8,128)(2,1)S(1)}, bf16[256,256]{1,0:T(8,128)(2,1)}, u32[]{:S(2)}) copy-start(bf16[256,256]{1,0:T(8,128)(2,1)} %param.7) | copy-start | bytes 393220
  191.2 193.6 %all-to-all-start.2 = ((f32[64,2,2,32,128]{4,3,2,1,0:T(8,128)}), f32[64,2,2,32,128]{4,3,2,1,0:T(8,128)}, u32[]{:S(2)}, u32[]{:S(2)}) async-start(f32[64,2,2,32,128]{4,3,2,1,0:T(8,128)} %bitcast.90), calls=%async_computation.2 | async-start | bytes 8388608 | tf_op jit(solution)/shard_map/all_to_all | solution.py:29
